TPU v7x, 32 devices: a whole 2x2x4 slice. The times are simulated.
32 devices in a mesh: groups: 2 (over x), heads: 4 (over y, core), seq: 4 (over z).
Axes of the slice: x: 2, y: 2, z: 4, core: 2. Of those that a mesh axis runs over, the one named last changes fastest.
Arguments:
- lin_query: bfloat16 [4096, 4096], P(('groups', 'seq'), 'heads'), parts along dimension 0, may hold values from -6 to 6
- lin_key: bfloat16 [4096, 4096], P(('groups', 'seq'), 'heads'), parts along dimension 0, may hold values from -6 to 6
- lin_value: bfloat16 [4096, 4096], P(('groups', 'seq'), 'heads'), parts along dimension 0, may hold values from -6 to 6
- log_decay: float32 [4096, 32], P(('groups', 'seq'), 'heads'), parts along dimension 0, may hold values from -1 to 0
- stream: bfloat16 [4096, 6144], P(('groups', 'seq'), 'heads'), parts along dimension 0, may hold values from -400 to 400
- out_weight: bfloat16 [4096, 6144], P('heads', 'seq'), may hold values from -0.125 to 0.125
- norm_gain: bfloat16 [6144], P('heads'), may hold values from 0.5 to 1.5
- query_weight: bfloat16 [6144, 4096], P('seq', 'heads'), may hold values from -12 to 12
- kv_weight: bfloat16 [4, 6144, 256], P(None, 'seq'), may hold values from -1 to 1
Outputs:
- stream_next: bfloat16 [4096, 6144], P(('groups', 'seq'), 'heads'), parts along dimension 0
- attended: bfloat16 [4096, 4096], P(('groups', 'seq'), 'heads'), parts along dimension 0
There are 2 independent parts, one for each index of `groups`. A program takes and returns all parts, laid end to end along the dimension named above; an argument that names none is the same for every part. Nothing has to cross between parts.
All inputs are finite; a program needn't handle non-finite values.
Results may differ from a plain program's by a relative error of at most 0.019.
Values may be sent and summed in bfloat16 or wider, within the bound.
No kernel may reach another device: no remote copies, remote signals or barrier semaphores. Data moves between devices by JAX's collectives and lax.ppermute only.
A program may use at most 128 MiB of HBM per device.

v0:
```python
import jax
import jax.numpy as jnp
from jax import lax
from jax.sharding import PartitionSpec as P

D = 6144
QUERY_HEADS = 32
KVH = 4
DH = 128
BLOCK = 256


def from_behind(value, axis, steps):
    count = lax.axis_size(axis)
    leading, last = (max(0, -steps), min(count, count - steps))
    return lax.ppermute(value, axis, [(source, source + steps) for source in range(leading, last)])


def lightning_block(kv_state, block_inputs):
    query_blk, key_blk, value_blk, decay_blk = block_inputs
    block_len = query_blk.shape[0]
    local_cum = jnp.cumsum(decay_blk, axis=0)
    causal_mask = (jnp.arange(block_len)[:, None] >= jnp.arange(block_len)[None, :])[:, :, None]
    decay_diff = local_cum[:, None, :] - local_cum[None, :, :]
    decays = jnp.where(causal_mask, jnp.exp(jnp.where(causal_mask, decay_diff, 0.0)), 0.0)
    scores = jnp.einsum("thd,shd->hts", query_blk, key_blk, preferred_element_type=jnp.float32)
    weights = (scores * jnp.transpose(decays, (2, 0, 1))).astype(jnp.bfloat16)
    intra_out = jnp.einsum("hts,shd->thd", weights, value_blk, preferred_element_type=jnp.float32)
    query_f = query_blk.astype(jnp.float32)
    inter_out = jnp.einsum(
        "thd,hde->the",
        query_f * jnp.exp(local_cum)[:, :, None],
        kv_state,
        precision=lax.Precision.HIGHEST,
    )
    tail_decay = jnp.exp(local_cum[-1][None, :] - local_cum)
    key_f = key_blk.astype(jnp.float32) * tail_decay[:, :, None]
    kv_state = jnp.exp(local_cum[-1])[:, None, None] * kv_state + jnp.einsum(
        "shd,she->hde", key_f, value_blk.astype(jnp.float32), precision=lax.Precision.HIGHEST
    )
    return (kv_state, intra_out + inter_out)


def shards_base(
    lin_query, lin_key, lin_value, log_decay, stream, out_weight, norm_gain, query_weight, kv_weight
):
    tok_rows = lin_query.shape[0]
    heads_here = log_decay.shape[1]
    head_width = heads_here * DH
    nblocks = tok_rows // BLOCK
    block_shape = (nblocks, BLOCK, heads_here, DH)
    inputs = (
        lin_query.reshape(block_shape),
        lin_key.reshape(block_shape),
        lin_value.reshape(block_shape),
        log_decay.reshape(nblocks, BLOCK, heads_here),
    )
    start_state = jnp.zeros((heads_here, DH, DH), jnp.float32)
    local_state, local_out = lax.scan(lightning_block, start_state, inputs)
    local_out = local_out.reshape(tok_rows, heads_here, DH)
    decay_total = jnp.sum(log_decay, axis=0)
    totals, states = (
        lax.all_gather(decay_total[None].astype(jnp.bfloat16), "seq", axis=0, tiled=True).astype(
            jnp.float32
        ),
        lax.all_gather(local_state[None].astype(jnp.bfloat16), "seq", axis=0, tiled=True).astype(
            jnp.float32
        ),
    )
    position = lax.axis_index("seq")
    device_order = jnp.arange(totals.shape[0])
    earlier = (device_order < position)[:, None]
    before = jnp.sum(jnp.where(earlier, totals, 0.0), axis=0)
    inclusive = jnp.cumsum(totals, axis=0)
    factors = jnp.where(earlier, jnp.exp(jnp.where(earlier, before[None, :] - inclusive, 0.0)), 0.0)
    incoming = jnp.einsum("jh,jhde->hde", factors, states, precision=lax.Precision.HIGHEST)
    running = jnp.cumsum(log_decay, axis=0)
    query_f = (
        lin_query.reshape(tok_rows, heads_here, DH).astype(jnp.float32)
        * jnp.exp(running)[:, :, None]
    )
    carried = jnp.einsum("thd,hde->the", query_f, incoming, precision=lax.Precision.HIGHEST)
    lin_raw = local_out + carried
    lin_out = (
        (lin_raw * lax.rsqrt(jnp.mean(lin_raw * lin_raw, axis=-1, keepdims=True) + 1e-06))
        .astype(jnp.bfloat16)
        .reshape(tok_rows, head_width)
    )
    branch = jnp.dot(
        lin_out,
        lax.all_gather(out_weight, "seq", axis=1, tiled=True),
        preferred_element_type=jnp.float32,
    )
    kv_group = lax.axis_index("heads") * heads_here // (QUERY_HEADS // KVH)
    kv_mine = lax.dynamic_index_in_dim(kv_weight, kv_group, 0, keepdims=False)
    query_rows, kv_rows = (
        lax.all_gather(query_weight, "seq", axis=0, tiled=True),
        lax.all_gather(kv_mine, "seq", axis=0, tiled=True),
    )
    projection = jnp.concatenate([query_rows, kv_rows], axis=1)
    own_sum = lax.psum_scatter(
        branch.astype(jnp.bfloat16), "heads", scatter_dimension=1, tiled=True
    ).astype(jnp.float32)
    mixed_sum = stream.astype(jnp.float32) + own_sum
    stream_next = mixed_sum.astype(jnp.bfloat16)
    total_sq = lax.psum(jnp.sum(mixed_sum * mixed_sum, axis=1), "heads")
    normed = (
        mixed_sum
        * lax.rsqrt(total_sq / D + 1e-05)[:, None]
        * norm_gain.astype(jnp.float32)[None, :]
    ).astype(jnp.bfloat16)
    projected = jnp.dot(
        lax.all_gather(normed, "heads", axis=1, tiled=True),
        projection,
        preferred_element_type=jnp.float32,
    )
    projected = projected.astype(jnp.bfloat16)
    queries = projected[:, :head_width].reshape(tok_rows, heads_here, DH)
    keys_values = projected[:, head_width:]
    position = lax.axis_index("seq")
    query_pos = position * tok_rows + jnp.arange(tok_rows)
    score_scale = float(DH) ** (-0.5)

    def attend(state_in, kv_block, key_start):
        old_max, row_total, weighted = state_in
        key_count = kv_block.shape[0]
        key_part = kv_block[:, :DH]
        value_part = kv_block[:, DH:]
        scores = (
            jnp.einsum("thd,sd->hts", queries, key_part, preferred_element_type=jnp.float32)
            * score_scale
        )
        key_pos = key_start + jnp.arange(key_count)
        allowed = ((key_pos[None, :] <= query_pos[:, None]) & (key_pos[None, :] >= 0))[None, :, :]
        scores = jnp.where(allowed, scores, -1e30)
        new_max = jnp.maximum(old_max, jnp.max(scores, axis=-1))
        expos = jnp.where(allowed, jnp.exp(scores - new_max[:, :, None]), 0.0)
        rescale = jnp.exp(old_max - new_max)
        row_total = row_total * rescale + jnp.sum(expos, axis=-1)
        prob_bf16 = expos.astype(jnp.bfloat16)
        weighted = weighted * rescale[:, :, None] + jnp.einsum(
            "hts,sd->htd", prob_bf16, value_part, preferred_element_type=jnp.float32
        )
        return (new_max, row_total, weighted)

    initial = (
        jnp.full((heads_here, tok_rows), -1e30, jnp.float32),
        jnp.zeros((heads_here, tok_rows), jnp.float32),
        jnp.zeros((heads_here, tok_rows, DH), jnp.float32),
    )
    first_state = attend(initial, keys_values, position * tok_rows)
    seq_count = lax.axis_size("seq")

    def cycle_turn(turn_index, loop_state):
        moving, inner_state = loop_state
        moving = from_behind(moving, "seq", 1)
        source = position - turn_index
        return (moving, attend(inner_state, moving, source * tok_rows))

    _, final_state = lax.fori_loop(1, seq_count, cycle_turn, (keys_values, first_state))
    _, row_total, weighted = final_state
    attended = (
        jnp.transpose(weighted / row_total[:, :, None], (1, 0, 2))
        .reshape(tok_rows, head_width)
        .astype(jnp.bfloat16)
    )
    return (stream_next, attended)


def lightning_local(lin_query, lin_key, lin_value, log_decay):
    tok_rows = lin_query.shape[0]
    heads_here = log_decay.shape[1]
    nblocks = tok_rows // BLOCK
    shape4 = (tok_rows, heads_here, DH)
    q4, k4, v4 = (x.reshape(shape4) for x in (lin_query, lin_key, lin_value))
    state = jnp.zeros((heads_here, DH, DH), jnp.float32)
    outs = []
    for blk in range(nblocks):
        rows = slice(blk * BLOCK, (blk + 1) * BLOCK)
        state, out = lightning_block(state, (q4[rows], k4[rows], v4[rows], log_decay[rows]))
        outs.append(out)
    local_out = jnp.concatenate(outs, axis=0)
    decay_total = jnp.sum(log_decay, axis=0)
    packed = jnp.concatenate([state.reshape(-1), decay_total]).astype(jnp.bfloat16)
    gathered = lax.all_gather(packed, "seq", axis=0, tiled=False).astype(jnp.float32)
    state_size = state.size
    states = gathered[:, :state_size].reshape((-1,) + state.shape)
    totals = gathered[:, state_size:]
    position = lax.axis_index("seq")
    device_order = jnp.arange(totals.shape[0])
    earlier = (device_order < position)[:, None]
    before = jnp.sum(jnp.where(earlier, totals, 0.0), axis=0)
    inclusive = jnp.cumsum(totals, axis=0)
    factors = jnp.where(earlier, jnp.exp(jnp.where(earlier, before[None, :] - inclusive, 0.0)), 0.0)
    incoming = jnp.einsum("jh,jhde->hde", factors, states, precision=lax.Precision.HIGHEST)
    running = jnp.cumsum(log_decay, axis=0)
    query_f = q4.astype(jnp.float32) * jnp.exp(running)[:, :, None]
    carried = jnp.einsum("thd,hde->the", query_f, incoming, precision=lax.Precision.HIGHEST)
    lin_raw = local_out + carried
    lin_out = (
        (lin_raw * lax.rsqrt(jnp.mean(lin_raw * lin_raw, axis=-1, keepdims=True) + 1e-06))
        .astype(jnp.bfloat16)
        .reshape(tok_rows, heads_here * DH)
    )
    return lin_out


def attend_block(queries, query_pos, state_in, kv_block, key_start):
    old_max, row_total, weighted = state_in
    key_count = kv_block.shape[0]
    key_part = kv_block[:, :DH]
    value_part = kv_block[:, DH:]
    score_scale = float(DH) ** (-0.5)
    scores = (
        jnp.einsum("thd,sd->hts", queries, key_part, preferred_element_type=jnp.float32)
        * score_scale
    )
    key_pos = key_start + jnp.arange(key_count)
    allowed = ((key_pos[None, :] <= query_pos[:, None]) & (key_pos[None, :] >= 0))[None, :, :]
    scores = jnp.where(allowed, scores, -1e30)
    new_max = jnp.maximum(old_max, jnp.max(scores, axis=-1))
    expos = jnp.where(allowed, jnp.exp(scores - new_max[:, :, None]), 0.0)
    rescale = jnp.exp(old_max - new_max)
    row_total = row_total * rescale + jnp.sum(expos, axis=-1)
    prob_bf16 = expos.astype(jnp.bfloat16)
    weighted = weighted * rescale[:, :, None] + jnp.einsum(
        "hts,sd->htd", prob_bf16, value_part, preferred_element_type=jnp.float32
    )
    return (new_max, row_total, weighted)


def shards_fast(
    lin_query, lin_key, lin_value, log_decay, stream, out_weight, norm_gain, query_weight, kv_weight
):
    n_heads = lax.axis_size("heads")
    n_seq = lax.axis_size("seq")
    tok_rows = lin_query.shape[0]
    heads_here = log_decay.shape[1]
    head_width = heads_here * DH
    mine_a = lax.axis_index("heads")
    mine_b = lax.axis_index("seq")
    swap = [(x * n_seq + y, y * n_seq + x) for x in range(n_heads) for y in range(n_seq)]
    stream_t = lax.ppermute(stream, ("heads", "seq"), swap)
    lin_out = lightning_local(lin_query, lin_key, lin_value, log_decay)
    lin_all = lax.all_gather(lin_out, "seq", axis=0, tiled=True)
    part = jnp.dot(lin_all, out_weight, preferred_element_type=jnp.float32).astype(jnp.bfloat16)
    own_sum = lax.psum_scatter(part, "heads", scatter_dimension=0, tiled=True)
    mixed_sum = stream_t.astype(jnp.float32) + own_sum.astype(jnp.float32)
    stream_next = lax.ppermute(mixed_sum.astype(jnp.bfloat16), ("heads", "seq"), swap)
    total_sq = lax.psum(jnp.sum(mixed_sum * mixed_sum, axis=1), "seq")
    cols = mixed_sum.shape[1]
    gain_all = lax.all_gather(norm_gain, "heads", axis=0, tiled=True)
    gain_b = lax.dynamic_slice_in_dim(gain_all, mine_b * cols, cols)
    normed = (
        mixed_sum * lax.rsqrt(total_sq / D + 1e-05)[:, None] * gain_b.astype(jnp.float32)[None, :]
    ).astype(jnp.bfloat16)
    normed_all = lax.all_gather(normed, "heads", axis=0, tiled=True)
    kv_group = mine_a * heads_here // (QUERY_HEADS // KVH)
    kv_mine = lax.dynamic_index_in_dim(kv_weight, kv_group, 0, keepdims=False)
    projection = jnp.concatenate([query_weight, kv_mine], axis=1)
    part2 = jnp.dot(normed_all, projection, preferred_element_type=jnp.float32).astype(jnp.bfloat16)
    reduced = lax.psum_scatter(part2, "seq", scatter_dimension=0, tiled=True)
    queries = reduced[:, :head_width].reshape(tok_rows, heads_here, DH)
    kv_own = reduced[:, head_width:]
    query_pos = mine_b * tok_rows + jnp.arange(tok_rows)
    state = (
        jnp.full((heads_here, tok_rows), -1e30, jnp.float32),
        jnp.zeros((heads_here, tok_rows), jnp.float32),
        jnp.zeros((heads_here, tok_rows, DH), jnp.float32),
    )
    earlier_kv = [from_behind(kv_own, "seq", dist) for dist in range(1, n_seq)]
    state = attend_block(queries, query_pos, state, kv_own, mine_b * tok_rows)
    for dist in range(1, n_seq):
        key_start = (mine_b - dist) * tok_rows
        state = attend_block(queries, query_pos, state, earlier_kv[dist - 1], key_start)
    _, row_total, weighted = state
    attended = (
        jnp.transpose(weighted / row_total[:, :, None], (1, 0, 2))
        .reshape(tok_rows, head_width)
        .astype(jnp.bfloat16)
    )
    return (stream_next, attended)


def solution(mesh):
    n_heads = mesh.shape["heads"]
    n_seq = mesh.shape["seq"]
    fast_ok = n_heads == n_seq and QUERY_HEADS % n_heads == 0
    if fast_ok:
        heads_here = QUERY_HEADS // n_heads
        fast_ok = QUERY_HEADS // KVH % heads_here == 0 and D % n_seq == 0
    shards = shards_fast if fast_ok else shards_base
    return jax.shard_map(
        shards,
        mesh=mesh,
        in_specs=(
            P(("groups", "seq"), "heads"),
            P(("groups", "seq"), "heads"),
            P(("groups", "seq"), "heads"),
            P(("groups", "seq"), "heads"),
            P(("groups", "seq"), "heads"),
            P("heads", "seq"),
            P("heads"),
            P("seq", "heads"),
            P(None, "seq", None),
        ),
        out_specs=(P(("groups", "seq"), "heads"), P(("groups", "seq"), "heads")),
        check_vma=False,
    )
```

profile of v0, /device:TPU:28, one launch (start us, length us, event | category | flops | bytes accessed | tf_op | source)
XLA Modules:
  0.0 567.0 jit_solution(838677574151914979)
XLA Ops:
  11.2 2.2 fusion.108
  13.4 2.1 copy.237
  15.5 2.2 fusion.109
  17.7 2.0 copy.238
  19.8 2.0 copy.239
  21.8 2.0 copy.240
  23.8 1.9 convolution_add_fusion.1
  26.5 1.9 fusion.43
  29.3 3.3 maximum_bitcast_fusion
  33.2 2.2 fusion.107
  36.7 2.1 copy.242
  38.8 2.0 copy.241
  41.0 3.4 fusion.38
  44.4 4.3 fusion.42
  48.7 3.3 fusion.40
  52.0 4.5 fusion.41
  56.5 20.7 %all-gather.10.cloned.1.call-done = bf16[4,1,131080]{2,1,0:T(2,128)(2,1)} async-done(((bf16[1,1,131080]{2,1,0:T(2,128)(2,1)}), bf16[4,1,131080]{2,1,0:T(2,128)(2,1)}) %all-gather.10.cloned.1.call-update) | async-done | bytes 1048656 | tf_op jit(solution)/shard_map/all_gather | solution.py:185
  77.2 2.6 copy.280
  83.5 2.7 multiply_reduce_fusion.2
  87.7 2.3 copy.188
  90.0 11.4 %reduce-scatter.3.cloned.1.call-start = ((), (), s32[]{:S(2)}) async-start(), calls=%async_computation.3 | async-start | bytes 7864320 | tf_op jit(solution)/shard_map/reduce_scatter | solution.py:247
  101.4 67.9 %all-gather.6.cloned.1.call-done = bf16[2048,1024]{0,1:T(8,128)(2,1)} async-done(((bf16[512,1024]{0,1:T(8,128)(2,1)}), bf16[2048,1024]{0,1:T(8,128)(2,1)}) %all-gather.6.cloned.1.call-update) | async-done | bytes 4194320 | tf_op jit(solution)/shard_map/all_gather | solution.py:245
  169.3 11.0 %convolution_convert_fusion.1 = bf16[2048,1536]{1,0:T(8,128)(2,1)} fusion(bf16[2048,1024]{0,1:T(8,128)(2,1)} %all-gather.6.cloned.1.call-done, bf16[1024,1536]{1,0:T(8,128)(2,1)S(1)} %copy-done), kind=kOutput, calls=%fused_computation.9 | convolution fusion | flops 6445596672 | bytes 13631488 | tf_op jit(solution)/shard_map/dot_general | solution.py:246
  180.4 2.8 collective-permute-start
  183.2 6.2 %all-gather.1 = bf16[4,1,1536]{2,1,0:T(2,128)(2,1)S(1)} all-gather(bf16[1,1,1536]{2,1,0:T(2,128)(2,1)S(1)} %reshape.428), channel_id=1, replica_groups=mesh['groups'=2,'heads'=4,'seq'=4] {'heads'}, dimensions={0}, use_global_device_ids=true | all-gather | bytes 15360 | tf_op jit(solution)/shard_map/all_gather | solution.py:252
  189.6 30.6 %collective-permute-done = bf16[512,1536]{1,0:T(8,128)(2,1)S(1)} collective-permute-done((bf16[512,1536]{1,0:T(8,128)(2,1)}, bf16[512,1536]{1,0:T(8,128)(2,1)S(1)}, u32[]{:S(2)}, u32[]{:S(2)}) %collective-permute-start) | collective-permute-done | bytes 1572896 | tf_op jit(solution)/shard_map/ppermute | solution.py:243
  220.2 40.5 %reduce-scatter.3.cloned.1.call-done = bf16[512,1536]{1,0:T(8,128)(2,1)} async-done(((bf16[2048,1536]{1,0:T(8,128)(2,1)}), bf16[512,1536]{1,0:T(8,128)(2,1)}) %reduce-scatter.3.cloned.1.call-update) | async-done | bytes 1572880 | tf_op jit(solution)/shard_map/reduce_scatter | solution.py:247
  260.7 2.1 multiply_reduce_fusion
  262.8 12.8 %psum.7 = f32[512]{0:T(512)S(1)} all-reduce(f32[512]{0:T(512)S(1)} %multiply_reduce_fusion), channel_id=1, replica_groups=mesh['groups'=2,'heads'=4,'seq'=4] {'seq'}, use_global_device_ids=true, to_apply=%region_12.13 | all-reduce | flops 512 | bytes 4096 | tf_op jit(solution)/shard_map/psum | solution.py:250
  275.6 2.3 multiply_convert_fusion
  279.1 45.4 %all-gather.8.cloned.1.call-done = bf16[2048,1536]{1,0:T(8,128)(2,1)} async-done(((bf16[512,1536]{1,0:T(8,128)(2,1)}), bf16[2048,1536]{1,0:T(8,128)(2,1)}) %all-gather.8.cloned.1.call-update) | async-done | bytes 6291472 | tf_op jit(solution)/shard_map/all_gather | solution.py:257
  324.5 12.9 %convolution_convert_fusion = bf16[2048,1280]{1,0:T(8,128)(2,1)} fusion(bf16[2048,1536]{1,0:T(8,128)(2,1)} %all-gather.8.cloned.1.call-done, bf16[1536,256]{1,0:T(8,128)(2,1)S(1)} %dynamic-slice_bitcast_fusion, bf16[1536,1024]{1,0:T(8,128)(2,1)} %param.16), kind=kOutput, calls=%fused_computation.8 | convolution fusion | flops 8063549440 | bytes 15466496 | tf_op jit(solution)/shard_map/dot_general | solution.py:261
  338.8 2.3 collective-permute-start.1
  342.9 101.0 %collective-permute-done.1 = bf16[512,1536]{1,0:T(8,128)(2,1)S(1)} collective-permute-done((bf16[512,1536]{1,0:T(8,128)(2,1)S(1)}, bf16[512,1536]{1,0:T(8,128)(2,1)S(1)}, u32[]{:S(2)}, u32[]{:S(2)}) %collective-permute-start.1) | collective-permute-done | bytes 1572896 | tf_op jit(solution)/shard_map/ppermute | solution.py:249
  443.9 41.8 %reduce-scatter.5.cloned.1.call-done = bf16[512,1280]{1,0:T(8,128)(2,1)} async-done(((bf16[2048,1280]{1,0:T(8,128)(2,1)}), bf16[512,1280]{1,0:T(8,128)(2,1)}) %reduce-scatter.5.cloned.1.call-update) | async-done | bytes 1310736 | tf_op jit(solution)/shard_map/reduce_scatter | solution.py:262
  490.6 3.0 fusion
  493.6 15.3 %collective-permute-done.2 = bf16[512,256]{1,0:T(8,128)(2,1)S(1)} collective-permute-done((bf16[512,256]{1,0:T(8,128)(2,1)S(1)}, bf16[512,256]{1,0:T(8,128)(2,1)S(1)}, u32[]{:S(2)}, u32[]{:S(2)}) %collective-permute-start.2) | collective-permute-done | bytes 262176 | tf_op jit(solution)/shard_map/ppermute | solution.py:16
  510.4 4.6 collective-permute-done.4
  516.6 9.7 %collective-permute-done.3 = bf16[512,256]{1,0:T(8,128)(2,1)S(1)} collective-permute-done((bf16[512,256]{1,0:T(8,128)(2,1)S(1)}, bf16[512,256]{1,0:T(8,128)(2,1)S(1)}, u32[]{:S(2)}, u32[]{:S(2)}) %collective-permute-start.3) | collective-permute-done | bytes 262176 | tf_op jit(solution)/shard_map/ppermute | solution.py:16
  526.2 4.8 fusion.2
  531.0 4.2 fusion.4
  535.2 6.3 %fusion.8 = (f32[8,512]{1,0:T(8,128)S(1)}, f32[8,512]{1,0:T(8,128)S(1)}) fusion(f32[512,512,8]{1,0,2:T(8,128)} %get-tuple-element.46, f32[8,512]{1,0:T(8,128)S(1)} %get-tuple-element.18, pred[512,512]{0,1:T(8,128)(4,1)S(1)} %copy-done.9, f32[8,512]{1,0:T(8,128)S(1)} %get-tuple-element.17, f32[512,512,8]{1,0,2:T(8,128)S(1)} %get-tuple-element.44, ...), kind=kLoop, calls=%fused_computation.18 | loop fusion | flops 20963328 | bytes 17367040 | tf_op jit(solution)/shard_map/reduce_sum | solution.py:224
  541.6 2.2 fusion.18
  543.8 2.2 fusion.16
  545.9 5.6 fusion.14
  551.5 3.8 fusion.31
  555.3 2.3 copy.201
  557.6 2.7 copy.282
  (99 shorter events, 25.5 us)
Async XLA Ops:
  7.2 162.2 %copy-start = (bf16[1024,1536]{1,0:T(8,128)(2,1)S(1)}, bf16[1024,1536]{1,0:T(8,128)(2,1)}, u32[]{:S(2)}) copy-start(bf16[1024,1536]{1,0:T(8,128)(2,1)} %param.14) | copy-start | bytes 9437188
  7.2 70.1 %all-gather.10.cloned.1.call-start = ((), (), s32[]{:S(2)}) async-start(), calls=%async_computation.6 | async-start | bytes 2624000 | tf_op jit(solution)/shard_map/all_gather | solution.py:185
  23.8 11.6 %copy-start.12 = (f32[512,8]{0,1:T(8,128)S(1)}, f32[512,8]{0,1:T(8,128)}, u32[]{:S(2)}) copy-start(f32[512,8]{0,1:T(8,128)} %param.12) | copy-start | bytes 49156
  25.7 0.8 copy-start.3
  32.6 136.7 %all-gather.6.cloned.1.call-start = ((), (), s32[]{:S(2)}) async-start(), calls=%async_computation.2 | async-start | bytes 5242880 | tf_op jit(solution)/shard_map/all_gather | solution.py:245
  81.3 1.9 copy-start.4
  81.3 1.9 copy-start.5
  81.3 2.2 copy-start.6
  90.0 170.7 %reduce-scatter.3.cloned.1.call-start = ((), (), s32[]{:S(2)}) async-start(), calls=%async_computation.3 | async-start | bytes 7864320 | tf_op jit(solution)/shard_map/reduce_scatter | solution.py:247
  180.3 2.8 copy-start.14
  180.3 144.2 %all-gather.8.cloned.1.call-start = ((), (), s32[]{:S(2)}) async-start(), calls=%async_computation.4 | async-start | bytes 7864320 | tf_op jit(solution)/shard_map/all_gather | solution.py:257
  180.4 39.8 %collective-permute-start = (bf16[512,1536]{1,0:T(8,128)(2,1)}, bf16[512,1536]{1,0:T(8,128)(2,1)S(1)}, u32[]{:S(2)}, u32[]{:S(2)}) collective-permute-start(bf16[512,1536]{1,0:T(8,128)(2,1)} %param.13), channel_id=1, source_target_pairs={{0,0},{1,4},{2,8},{3,12},{4,1},{5,5},{6,9},{7,13},{8,2},{9,6},{10,... | collective-permute-start | bytes 4718600 | tf_op jit(solution)/shard_map/ppermute | solution.py:243
  260.7 14.9 %copy-start.2 = (bf16[512,1536]{1,0:T(8,128)(2,1)S(1)}, bf16[512,1536]{1,0:T(8,128)(2,1)}, u32[]{:S(2)}) copy-start(bf16[512,1536]{1,0:T(8,128)(2,1)} %reduce-scatter.3.cloned.1.call-done) | copy-start | bytes 4718596
  277.9 207.8 %reduce-scatter.5.cloned.1.call-start = ((), (), s32[]{:S(2)}) async-start(), calls=%async_computation.5 | async-start | bytes 6553600 | tf_op jit(solution)/shard_map/reduce_scatter | solution.py:262
  337.4 1.4 copy-start.8
  338.8 105.1 %collective-permute-start.1 = (bf16[512,1536]{1,0:T(8,128)(2,1)S(1)}, bf16[512,1536]{1,0:T(8,128)(2,1)S(1)}, u32[]{:S(2)}, u32[]{:S(2)}) collective-permute-start(bf16[512,1536]{1,0:T(8,128)(2,1)S(1)} %copy-done.8), channel_id=1, source_target_pairs={{0,0},{1,4},{2,8},{3,12},{4,1},{5,5},{6,9},{7,13},{8,2},{9,6},{10,... | collective-permute-start | bytes 4718600 | tf_op jit(solution)/shard_map/ppermute | solution.py:249
  443.9 49.7 %copy-start.7 = (bf16[512,1536]{1,0:T(8,128)(2,1)}, bf16[512,1536]{1,0:T(8,128)(2,1)S(1)}, u32[]{:S(2)}) copy-start(bf16[512,1536]{1,0:T(8,128)(2,1)S(1)} %collective-permute-done.1) | copy-start | bytes 4718596
  486.6 22.2 %collective-permute-start.2 = (bf16[512,256]{1,0:T(8,128)(2,1)S(1)}, bf16[512,256]{1,0:T(8,128)(2,1)S(1)}, u32[]{:S(2)}, u32[]{:S(2)}) collective-permute-start(bf16[512,256]{1,0:T(8,128)(2,1)S(1)} %slice.154), channel_id=1, source_target_pairs={{0,1},{1,2},{2,3},{4,5},{5,6},{6,7},{8,9},{9,10},{10,11},{12,13},{... | collective-permute-start | bytes 786440 | tf_op jit(solution)/shard_map/ppermute | solution.py:16
  487.9 27.0 %collective-permute-start.4 = (bf16[512,256]{1,0:T(8,128)(2,1)S(1)}, bf16[512,256]{1,0:T(8,128)(2,1)S(1)}, u32[]{:S(2)}, u32[]{:S(2)}) collective-permute-start(bf16[512,256]{1,0:T(8,128)(2,1)S(1)} %slice.154), channel_id=1, source_target_pairs={{0,3},{4,7},{8,11},{12,15},{16,19},{20,23},{24,27},{28,31}} | collective-permute-start | bytes 786440 | tf_op jit(solution)/shard_map/ppermute | solution.py:16
  489.2 37.0 %collective-permute-start.3 = (bf16[512,256]{1,0:T(8,128)(2,1)S(1)}, bf16[512,256]{1,0:T(8,128)(2,1)S(1)}, u32[]{:S(2)}, u32[]{:S(2)}) collective-permute-start(bf16[512,256]{1,0:T(8,128)(2,1)S(1)} %slice.154), channel_id=1, source_target_pairs={{0,2},{1,3},{4,6},{5,7},{8,10},{9,11},{12,14},{13,15},{16,18},{17,... | collective-permute-start | bytes 786440 | tf_op jit(solution)/shard_map/ppermute | solution.py:16
  490.5 18.3 %copy-start.10 = (pred[512,512]{0,1:T(8,128)(4,1)S(1)}, pred[512,512]{0,1:T(8,128)(4,1)}, u32[]{:S(2)}) copy-start(pred[512,512]{0,1:T(8,128)(4,1)} %get-tuple-element.40) | copy-start | bytes 786436
  490.6 18.3 %copy-start.13 = (bf16[512,1280]{1,0:T(8,128)(2,1)S(1)}, bf16[512,1280]{1,0:T(8,128)(2,1)}, u32[]{:S(2)}) copy-start(bf16[512,1280]{1,0:T(8,128)(2,1)} %reduce-scatter.5.cloned.1.call-done) | copy-start | bytes 3932164
  515.0 11.2 %copy-start.9 = (pred[512,512]{0,1:T(8,128)(4,1)S(1)}, pred[512,512]{0,1:T(8,128)(4,1)}, u32[]{:S(2)}) copy-start(pred[512,512]{0,1:T(8,128)(4,1)} %get-tuple-element.39) | copy-start | bytes 786436
  526.2 4.8 copy-start.11
  551.5 8.7 %copy-start.1 = (bf16[1024,1536]{1,0:T(8,128)(2,1)S(1)}, bf16[1024,1536]{1,0:T(8,128)(2,1)}, u32[]{:S(2)}) copy-start(bf16[1024,1536]{1,0:T(8,128)(2,1)} %param.14) | copy-start | bytes 9437188
Sparse Core Ops, SparseCore 0:
  32.7 44.4 all-gather.9
  90.1 79.1 all-gather.5
  180.5 80.1 reduce-scatter.2
  278.0 46.4 all-gather.7
  337.5 148.1 reduce-scatter.4
where the time goes:
time: 571 us; the launch traced here: 567 us
  waiting for transfers between devices  378 us (66%)
  matrix products  70.3 us (12%)
  local copies, waits for them, and re-layouts  38.9 us (7%)
  other arithmetic  26 us (5%)
  starting transfers between devices  20.9 us (4%)
  blocking collectives  19 us (3%)
  between operations  14.4 us (3%)
    ppermute x1, waiting for transfers between devices, shards_fast(): lax.ppermute(mixed_sum.astype(jnp.bfloat16), ('heads', 'seq'), swap)  101 us
    all_gather x1, waiting for transfers between devices, shards_fast(): lin_all = lax.all_gather(lin_out, 'seq', axis=0, tiled=True)  67.9 us
    all_gather x1, waiting for transfers between devices, shards_fast(): normed_all = lax.all_gather(normed, 'heads', axis=0, tiled=True)  45.4 us
    reduce_scatter x1, waiting for transfers between devices, shards_fast(): reduced = lax.psum_scatter(part2, 'seq', scatter_dimension=0, tiled=True)  41.8 us
    reduce_scatter x1, waiting for transfers between devices, shards_fast(): own_sum = lax.psum_scatter(part, 'heads', scatter_dimension=0, tiled=True)  40.5 us
    ppermute x1, waiting for transfers between devices, shards_fast(): stream_t = lax.ppermute(stream, ('heads', 'seq'), swap)  30.6 us
    ppermute x3, waiting for transfers between devices, from_behind(): lax.ppermute(value, axis, [(source, source + steps) for source in range(l...  29.5 us
    unnamed x43, local copies, waits for them, and re-layouts  25.2 us
  transfers between devices with their start and end apart: 10, of which 10 were waited for; matrix products, arithmetic and copies ran while one was open for 6% of the time, Pallas kernels for 0%

commit v1 on v0

--- a/solution.py
+++ b/solution.py
@@ -8,6 +8,18 @@
 KVH = 4
 DH = 128
 BLOCK = 256
+
+
+def collect(x, axis, dim):
+    ways, here, hop = (lax.axis_size(axis), lax.axis_index(axis), x.shape[dim])
+    line, have = (x, 1)
+    while have < ways:
+        line = jnp.concatenate(
+            [line, lax.ppermute(line, axis, [(d, (d - have) % ways) for d in range(ways)])],
+            axis=dim,
+        )
+        have = 2 * have
+    return jnp.roll(line, here * hop, axis=dim)
 
 
 def from_behind(value, axis, steps):
@@ -242,7 +254,7 @@
     swap = [(x * n_seq + y, y * n_seq + x) for x in range(n_heads) for y in range(n_seq)]
     stream_t = lax.ppermute(stream, ("heads", "seq"), swap)
     lin_out = lightning_local(lin_query, lin_key, lin_value, log_decay)
-    lin_all = lax.all_gather(lin_out, "seq", axis=0, tiled=True)
+    lin_all = collect(lin_out, "seq", 0)
     part = jnp.dot(lin_all, out_weight, preferred_element_type=jnp.float32).astype(jnp.bfloat16)
     own_sum = lax.psum_scatter(part, "heads", scatter_dimension=0, tiled=True)
     mixed_sum = stream_t.astype(jnp.float32) + own_sum.astype(jnp.float32)

time: 571 us -> 628 us (1.100)
  waiting for transfers between devices: 378 us -> 428 us
  local copies, waits for them, and re-layouts: 38.9 us -> 46.6 us
    ppermute x0 -> x2, waiting for transfers between devices: none -> 114 us  [collect(): lax.ppermute(line, axis, [(d, (d - have) % ways) for d in range(ways)])]
    all_gather x1 -> x0, waiting for transfers between devices: 67.9 us -> none  [shards_fast(): lin_all = lax.all_gather(lin_out, 'seq', axis=0, tiled=True)]
    ppermute x0 -> x2, starting transfers between devices: none -> 13 us  [collect(): lax.ppermute(line, axis, [(d, (d - have) % ways) for d in range(ways)])]
    reduce_scatter x1, starting transfers between devices: 11.4 us -> 0.42 us  [shards_fast(): own_sum = lax.psum_scatter(part, 'heads', scatter_dimension=0, tiled=True)]
    unnamed x43 -> x54, local copies, waits for them, and re-layouts: 25.2 us -> 31.1 us
  transfers between devices with their start and end apart: 10 -> 11, of which waited for: 10 -> 11; matrix products, arithmetic and copies ran while one was open for 6% -> 6% of each run, Pallas kernels for 0% -> 0%
where the time goes in v1:
time: 628 us; the launch traced here: 623 us
  waiting for transfers between devices  428 us (68%)
  matrix products  68 us (11%)
  local copies, waits for them, and re-layouts  46.6 us (7%)
  other arithmetic  28.9 us (5%)
  starting transfers between devices  21.6 us (3%)
  blocking collectives  15.5 us (2%)
  between operations  14.4 us (2%)
    ppermute x2, waiting for transfers between devices, collect(): lax.ppermute(line, axis, [(d, (d - have) % ways) for d in range(ways)])  114 us
    ppermute x1, waiting for transfers between devices, shards_fast(): lax.ppermute(mixed_sum.astype(jnp.bfloat16), ('heads', 'seq'), swap)  101 us
    all_gather x1, waiting for transfers between devices, shards_fast(): normed_all = lax.all_gather(normed, 'heads', axis=0, tiled=True)  46.5 us
    reduce_scatter x1, waiting for transfers between devices, shards_fast(): own_sum = lax.psum_scatter(part, 'heads', scatter_dimension=0, tiled=True)  44.8 us
    reduce_scatter x1, waiting for transfers between devices, shards_fast(): reduced = lax.psum_scatter(part2, 'seq', scatter_dimension=0, tiled=True)  41.8 us
    unnamed x54, local copies, waits for them, and re-layouts  31.1 us
    ppermute x1, waiting for transfers between devices, shards_fast(): stream_t = lax.ppermute(stream, ('heads', 'seq'), swap)  29.6 us
    ppermute x3, waiting for transfers between devices, from_behind(): lax.ppermute(value, axis, [(source, source + steps) for source in range(l...  29.5 us
  transfers between devices with their start and end apart: 11, of which 11 were waited for; matrix products, arithmetic and copies ran while one was open for 6% of the time, Pallas kernels for 0%

profile of v1, /device:TPU:28, one launch (start us, length us, event | category | flops | bytes accessed | tf_op | source)
XLA Modules:
  0.0 623.1 jit_solution(10827499381382803574)
XLA Ops:
  11.2 2.2 fusion.110
  13.4 2.1 copy.237
  15.5 2.2 fusion.111
  17.7 2.0 copy.238
  19.8 2.0 copy.239
  21.8 2.0 copy.240
  29.3 3.3 maximum_bitcast_fusion
  33.2 2.2 fusion.109
  36.7 2.1 copy.242
  38.8 2.0 copy.241
  41.0 3.4 fusion.39
  44.4 4.3 fusion.43
  48.7 3.3 fusion.41
  52.0 4.5 fusion.42
  56.5 20.7 %all-gather.7.cloned.1.call-done = bf16[4,1,131080]{2,1,0:T(2,128)(2,1)} async-done(((bf16[1,1,131080]{2,1,0:T(2,128)(2,1)}), bf16[4,1,131080]{2,1,0:T(2,128)(2,1)}) %all-gather.7.cloned.1.call-update) | async-done | bytes 1048656 | tf_op jit(solution)/shard_map/all_gather | solution.py:197
  77.2 2.6 copy.280
  83.5 2.7 multiply_reduce_fusion.2
  87.7 2.3 copy.188
  90.0 13.0 %collective-permute-start.1 = (bf16[512,1024]{0,1:T(8,128)(2,1)}, bf16[512,1024]{0,1:T(8,128)(2,1)S(1)}, u32[]{:S(2)}, u32[]{:S(2)}) collective-permute-start(bf16[512,1024]{0,1:T(8,128)(2,1)} %bitcast.284), channel_id=1, source_target_pairs={{0,3},{1,0},{2,1},{3,2},{4,7},{5,4},{6,5},{7,6},{8,11},{9,8},{10,9... | collective-permute-start | bytes 3145736 | tf_op jit(solution)/shard_map/ppermute | solution.py:18
  103.0 25.6 %collective-permute-done.1 = bf16[512,1024]{0,1:T(8,128)(2,1)S(1)} collective-permute-done((bf16[512,1024]{0,1:T(8,128)(2,1)}, bf16[512,1024]{0,1:T(8,128)(2,1)S(1)}, u32[]{:S(2)}, u32[]{:S(2)}) %collective-permute-start.1) | collective-permute-done | bytes 1048608 | tf_op jit(solution)/shard_map/ppermute | solution.py:18
  129.5 2.9 pad_maximum_fusion
  135.3 88.4 %collective-permute-done.2 = bf16[1024,1024]{0,1:T(8,128)(2,1)} collective-permute-done((bf16[1024,1024]{0,1:T(8,128)(2,1)}, bf16[1024,1024]{0,1:T(8,128)(2,1)}, u32[]{:S(2)}, u32[]{:S(2)}) %collective-permute-start.2) | collective-permute-done | bytes 2097184 | tf_op jit(solution)/shard_map/ppermute | solution.py:18
  227.6 8.7 %convolution_convert_fusion.1 = bf16[2048,1536]{1,0:T(8,128)(2,1)} fusion(bf16[1024,1536]{1,0:T(8,128)(2,1)S(1)} %copy-done, bf16[4096,1024]{0,1:T(8,128)(2,1)S(1)} %constant_dynamic-update-slice_fusion, s32[]{:T(128)S(6)} %select_n.84), kind=kOutput, calls=%fused_computation.9 | convolution fusion | flops 6445596672 | bytes 13631492 | tf_op jit(solution)/shard_map/dot_general | solution.py:258
  236.3 1.9 collective-permute-start
  238.3 5.2 all-gather.1
  243.7 29.6 %collective-permute-done = bf16[512,1536]{1,0:T(8,128)(2,1)S(1)} collective-permute-done((bf16[512,1536]{1,0:T(8,128)(2,1)}, bf16[512,1536]{1,0:T(8,128)(2,1)S(1)}, u32[]{:S(2)}, u32[]{:S(2)}) %collective-permute-start) | collective-permute-done | bytes 1572896 | tf_op jit(solution)/shard_map/ppermute | solution.py:255
  273.3 44.8 %reduce-scatter.3.cloned.1.call-done = bf16[512,1536]{1,0:T(8,128)(2,1)} async-done(((bf16[2048,1536]{1,0:T(8,128)(2,1)}), bf16[512,1536]{1,0:T(8,128)(2,1)}) %reduce-scatter.3.cloned.1.call-update) | async-done | bytes 1572880 | tf_op jit(solution)/shard_map/reduce_scatter | solution.py:259
  318.1 2.1 multiply_reduce_fusion
  320.2 10.3 %psum.7 = f32[512]{0:T(512)S(1)} all-reduce(f32[512]{0:T(512)S(1)} %multiply_reduce_fusion), channel_id=1, replica_groups=mesh['groups'=2,'heads'=4,'seq'=4] {'seq'}, use_global_device_ids=true, to_apply=%region_12.13 | all-reduce | flops 512 | bytes 4096 | tf_op jit(solution)/shard_map/psum | solution.py:262
  330.5 2.3 multiply_convert_fusion
  334.1 46.5 %all-gather.5.cloned.1.call-done = bf16[2048,1536]{1,0:T(8,128)(2,1)} async-done(((bf16[512,1536]{1,0:T(8,128)(2,1)}), bf16[2048,1536]{1,0:T(8,128)(2,1)}) %all-gather.5.cloned.1.call-update) | async-done | bytes 6291472 | tf_op jit(solution)/shard_map/all_gather | solution.py:269
  380.6 12.9 %convolution_convert_fusion = bf16[2048,1280]{1,0:T(8,128)(2,1)} fusion(bf16[2048,1536]{1,0:T(8,128)(2,1)} %all-gather.5.cloned.1.call-done, bf16[1536,256]{1,0:T(8,128)(2,1)S(1)} %dynamic-slice_bitcast_fusion, bf16[1536,1024]{1,0:T(8,128)(2,1)} %param.16), kind=kOutput, calls=%fused_computation.8 | convolution fusion | flops 8063549440 | bytes 15466496 | tf_op jit(solution)/shard_map/dot_general | solution.py:273
  394.9 2.3 collective-permute-start.3
  399.0 101.0 %collective-permute-done.3 = bf16[512,1536]{1,0:T(8,128)(2,1)S(1)} collective-permute-done((bf16[512,1536]{1,0:T(8,128)(2,1)S(1)}, bf16[512,1536]{1,0:T(8,128)(2,1)S(1)}, u32[]{:S(2)}, u32[]{:S(2)}) %collective-permute-start.3) | collective-permute-done | bytes 1572896 | tf_op jit(solution)/shard_map/ppermute | solution.py:261
  500.0 41.8 %reduce-scatter.5.cloned.1.call-done = bf16[512,1280]{1,0:T(8,128)(2,1)} async-done(((bf16[2048,1280]{1,0:T(8,128)(2,1)}), bf16[512,1280]{1,0:T(8,128)(2,1)}) %reduce-scatter.5.cloned.1.call-update) | async-done | bytes 1310736 | tf_op jit(solution)/shard_map/reduce_scatter | solution.py:274
  546.7 3.0 fusion
  549.7 15.3 %collective-permute-done.4 = bf16[512,256]{1,0:T(8,128)(2,1)S(1)} collective-permute-done((bf16[512,256]{1,0:T(8,128)(2,1)S(1)}, bf16[512,256]{1,0:T(8,128)(2,1)S(1)}, u32[]{:S(2)}, u32[]{:S(2)}) %collective-permute-start.4) | collective-permute-done | bytes 262176 | tf_op jit(solution)/shard_map/ppermute | solution.py:28
  566.5 4.6 collective-permute-done.6
  572.6 9.7 %collective-permute-done.5 = bf16[512,256]{1,0:T(8,128)(2,1)S(1)} collective-permute-done((bf16[512,256]{1,0:T(8,128)(2,1)S(1)}, bf16[512,256]{1,0:T(8,128)(2,1)S(1)}, u32[]{:S(2)}, u32[]{:S(2)}) %collective-permute-start.5) | collective-permute-done | bytes 262176 | tf_op jit(solution)/shard_map/ppermute | solution.py:28
  582.3 4.8 fusion.2
  587.1 4.2 fusion.4
  591.3 6.3 %fusion.8 = (f32[8,512]{1,0:T(8,128)S(1)}, f32[8,512]{1,0:T(8,128)S(1)}) fusion(f32[512,512,8]{1,0,2:T(8,128)} %get-tuple-element.46, f32[8,512]{1,0:T(8,128)S(1)} %get-tuple-element.18, pred[512,512]{0,1:T(8,128)(4,1)S(1)} %copy-done.12, f32[8,512]{1,0:T(8,128)S(1)} %get-tuple-element.17, f32[512,512,8]{1,0,2:T(8,128)S(1)} %get-tuple-element.44, ...), kind=kLoop, calls=%fused_computation.18 | loop fusion | flops 20963328 | bytes 17367040 | tf_op jit(solution)/shard_map/reduce_sum | solution.py:236
  597.7 2.2 fusion.19
  599.9 2.2 fusion.17
  602.0 5.6 fusion.15
  607.6 3.8 fusion.32
  611.4 2.3 copy.201
  613.7 2.7 copy.287
  (113 shorter events, 36.9 us)
Async XLA Ops:
  7.2 220.4 %copy-start = (bf16[1024,1536]{1,0:T(8,128)(2,1)S(1)}, bf16[1024,1536]{1,0:T(8,128)(2,1)}, u32[]{:S(2)}) copy-start(bf16[1024,1536]{1,0:T(8,128)(2,1)} %param.14) | copy-start | bytes 9437188
  7.2 70.1 %all-gather.7.cloned.1.call-start = ((), (), s32[]{:S(2)}) async-start(), calls=%async_computation.5 | async-start | bytes 2624000 | tf_op jit(solution)/shard_map/all_gather | solution.py:197
  23.8 11.6 %copy-start.15 = (f32[512,8]{0,1:T(8,128)S(1)}, f32[512,8]{0,1:T(8,128)}, u32[]{:S(2)}) copy-start(f32[512,8]{0,1:T(8,128)} %param.12) | copy-start | bytes 49156
  25.7 0.8 copy-start.6
  32.6 285.5 %reduce-scatter.3.cloned.1.call-start = ((), (), s32[]{:S(2)}) async-start(), calls=%async_computation.2 | async-start | bytes 7864320 | tf_op jit(solution)/shard_map/reduce_scatter | solution.py:259
  81.3 1.9 copy-start.7
  81.3 1.9 copy-start.8
  81.3 2.2 copy-start.9
  90.0 38.5 %collective-permute-start.1 = (bf16[512,1024]{0,1:T(8,128)(2,1)}, bf16[512,1024]{0,1:T(8,128)(2,1)S(1)}, u32[]{:S(2)}, u32[]{:S(2)}) collective-permute-start(bf16[512,1024]{0,1:T(8,128)(2,1)} %bitcast.284), channel_id=1, source_target_pairs={{0,3},{1,0},{2,1},{3,2},{4,7},{5,4},{6,5},{7,6},{8,11},{9,8},{10,9... | collective-permute-start | bytes 3145736 | tf_op jit(solution)/shard_map/ppermute | solution.py:18
  128.5 1.0 copy-start.3
  132.4 91.3 %collective-permute-start.2 = (bf16[1024,1024]{0,1:T(8,128)(2,1)}, bf16[1024,1024]{0,1:T(8,128)(2,1)}, u32[]{:S(2)}, u32[]{:S(2)}) collective-permute-start(bf16[1024,1024]{0,1:T(8,128)(2,1)} %pad_maximum_fusion), channel_id=1, source_target_pairs={{0,2},{1,3},{2,0},{3,1},{4,6},{5,7},{6,4},{7,5},{8,10},{9,11},{10,... | collective-permute-start | bytes 6291464 | tf_op jit(solution)/shard_map/ppermute | solution.py:18
  132.4 93.1 %copy-start.2 = (bf16[512,8,128]{0,2,1:T(8,128)(2,1)S(1)}, bf16[512,8,128]{0,2,1:T(8,128)(2,1)}, u32[]{:S(2)}) copy-start(bf16[512,8,128]{0,2,1:T(8,128)(2,1)} %copy.188) | copy-start | bytes 3145732
  133.8 91.8 %copy-start.4 = (bf16[512,1024]{0,1:T(8,128)(2,1)S(1)}, bf16[512,1024]{0,1:T(8,128)(2,1)}, u32[]{:S(2)}) copy-start(bf16[512,1024]{0,1:T(8,128)(2,1)} %copy-done.3) | copy-start | bytes 3145732
  236.2 2.0 copy-start.17
  236.3 144.3 %all-gather.5.cloned.1.call-start = ((), (), s32[]{:S(2)}) async-start(), calls=%async_computation.3 | async-start | bytes 7864320 | tf_op jit(solution)/shard_map/all_gather | solution.py:269
  236.3 36.9 %collective-permute-start = (bf16[512,1536]{1,0:T(8,128)(2,1)}, bf16[512,1536]{1,0:T(8,128)(2,1)S(1)}, u32[]{:S(2)}, u32[]{:S(2)}) collective-permute-start(bf16[512,1536]{1,0:T(8,128)(2,1)} %param.13), channel_id=1, source_target_pairs={{0,0},{1,4},{2,8},{3,12},{4,1},{5,5},{6,9},{7,13},{8,2},{9,6},{10,... | collective-permute-start | bytes 4718600 | tf_op jit(solution)/shard_map/ppermute | solution.py:255
  318.1 12.4 %copy-start.5 = (bf16[512,1536]{1,0:T(8,128)(2,1)S(1)}, bf16[512,1536]{1,0:T(8,128)(2,1)}, u32[]{:S(2)}) copy-start(bf16[512,1536]{1,0:T(8,128)(2,1)} %reduce-scatter.3.cloned.1.call-done) | copy-start | bytes 4718596
  332.8 208.9 %reduce-scatter.5.cloned.1.call-start = ((), (), s32[]{:S(2)}) async-start(), calls=%async_computation.4 | async-start | bytes 6553600 | tf_op jit(solution)/shard_map/reduce_scatter | solution.py:274
  393.5 1.4 copy-start.11
  394.9 105.1 %collective-permute-start.3 = (bf16[512,1536]{1,0:T(8,128)(2,1)S(1)}, bf16[512,1536]{1,0:T(8,128)(2,1)S(1)}, u32[]{:S(2)}, u32[]{:S(2)}) collective-permute-start(bf16[512,1536]{1,0:T(8,128)(2,1)S(1)} %copy-done.11), channel_id=1, source_target_pairs={{0,0},{1,4},{2,8},{3,12},{4,1},{5,5},{6,9},{7,13},{8,2},{9,6},{10,... | collective-permute-start | bytes 4718600 | tf_op jit(solution)/shard_map/ppermute | solution.py:261
  500.0 49.7 %copy-start.10 = (bf16[512,1536]{1,0:T(8,128)(2,1)}, bf16[512,1536]{1,0:T(8,128)(2,1)S(1)}, u32[]{:S(2)}) copy-start(bf16[512,1536]{1,0:T(8,128)(2,1)S(1)} %collective-permute-done.3) | copy-start | bytes 4718596
  542.7 22.2 %collective-permute-start.4 = (bf16[512,256]{1,0:T(8,128)(2,1)S(1)}, bf16[512,256]{1,0:T(8,128)(2,1)S(1)}, u32[]{:S(2)}, u32[]{:S(2)}) collective-permute-start(bf16[512,256]{1,0:T(8,128)(2,1)S(1)} %slice.154), channel_id=1, source_target_pairs={{0,1},{1,2},{2,3},{4,5},{5,6},{6,7},{8,9},{9,10},{10,11},{12,13},{... | collective-permute-start | bytes 786440 | tf_op jit(solution)/shard_map/ppermute | solution.py:28
  544.0 27.0 %collective-permute-start.6 = (bf16[512,256]{1,0:T(8,128)(2,1)S(1)}, bf16[512,256]{1,0:T(8,128)(2,1)S(1)}, u32[]{:S(2)}, u32[]{:S(2)}) collective-permute-start(bf16[512,256]{1,0:T(8,128)(2,1)S(1)} %slice.154), channel_id=1, source_target_pairs={{0,3},{4,7},{8,11},{12,15},{16,19},{20,23},{24,27},{28,31}} | collective-permute-start | bytes 786440 | tf_op jit(solution)/shard_map/ppermute | solution.py:28
  545.3 37.0 %collective-permute-start.5 = (bf16[512,256]{1,0:T(8,128)(2,1)S(1)}, bf16[512,256]{1,0:T(8,128)(2,1)S(1)}, u32[]{:S(2)}, u32[]{:S(2)}) collective-permute-start(bf16[512,256]{1,0:T(8,128)(2,1)S(1)} %slice.154), channel_id=1, source_target_pairs={{0,2},{1,3},{4,6},{5,7},{8,10},{9,11},{12,14},{13,15},{16,18},{17,... | collective-permute-start | bytes 786440 | tf_op jit(solution)/shard_map/ppermute | solution.py:28
  546.6 18.3 %copy-start.13 = (pred[512,512]{0,1:T(8,128)(4,1)S(1)}, pred[512,512]{0,1:T(8,128)(4,1)}, u32[]{:S(2)}) copy-start(pred[512,512]{0,1:T(8,128)(4,1)} %get-tuple-element.40) | copy-start | bytes 786436
  546.7 18.3 %copy-start.16 = (bf16[512,1280]{1,0:T(8,128)(2,1)S(1)}, bf16[512,1280]{1,0:T(8,128)(2,1)}, u32[]{:S(2)}) copy-start(bf16[512,1280]{1,0:T(8,128)(2,1)} %reduce-scatter.5.cloned.1.call-done) | copy-start | bytes 3932164
  571.1 11.2 %copy-start.12 = (pred[512,512]{0,1:T(8,128)(4,1)S(1)}, pred[512,512]{0,1:T(8,128)(4,1)}, u32[]{:S(2)}) copy-start(pred[512,512]{0,1:T(8,128)(4,1)} %get-tuple-element.39) | copy-start | bytes 786436
  582.3 4.8 copy-start.14
  607.6 8.7 %copy-start.1 = (bf16[1024,1536]{1,0:T(8,128)(2,1)S(1)}, bf16[1024,1536]{1,0:T(8,128)(2,1)}, u32[]{:S(2)}) copy-start(bf16[1024,1536]{1,0:T(8,128)(2,1)} %param.14) | copy-start | bytes 9437188
Sparse Core Ops, SparseCore 0:
  32.7 44.4 all-gather.6
  236.4 81.6 reduce-scatter.2
  333.0 47.5 all-gather.4
  393.6 148.1 reduce-scatter.4
